TPU v7x, 256 devices: a whole 4x4x8 slice. The times are simulated.
256 devices in a mesh: row: 16 (over x, z_hi, core), col: 4 (over y), rep: 4 (over z_lo).
Axes of the slice: x: 4, y: 4, z: 8 (z_hi: 2, z_lo: 4; z = z_hi * 4 + z_lo), core: 2. Of those that a mesh axis runs over, the one named last changes fastest.
Arguments:
- integrals: bfloat16 [8, 32, 60, 128, 128], P(None, 'row', 'rep', 'col'), may hold values from -0.0625 to 0.0625
- amplitudes: bfloat16 [8, 16, 60, 128, 128], P(None, 'col', 'rep', 'row'), may hold values from -6 to 6
- virt_count: int32 [8], replicated, may hold values from 76 to 128, as said below
- occ_irrep: int32 [60], replicated, may hold values from 0 to 7
Outputs:
- cycle: bfloat16 [8, 32, 128, 16, 128], P('rep', 'row', None, 'col')
Inputs may be any that keep to these rules, and one draw needn't show every extreme that they name: `virt_count`: one irrep has exactly 128 virtual orbitals.
All inputs are finite; a program needn't handle non-finite values.
Results may differ from a plain program's by a relative error of at most 0.001.
Values may be sent and summed in bfloat16 or wider, within the bound.
No kernel may reach another device: no remote copies, remote signals or barrier semaphores. Data moves between devices by JAX's collectives and lax.ppermute only.
A program may use at most 128 MiB of HBM per device.

v0:
```python
import jax
import jax.numpy as jnp
from jax import lax
from jax.sharding import PartitionSpec as P


def contract(w_part, t_part):
    w_full = lax.all_gather(w_part, "col", axis=3, tiled=True)
    return jnp.einsum(
        "gikca,gjkcb->giajb",
        w_full,
        lax.all_gather(t_part, "row", axis=3, tiled=True),
        preferred_element_type=jnp.float32,
    )


def body(integrals, amplitudes, virt_count, occ_irrep):
    ngroup = integrals.shape[0]
    k_local = integrals.shape[2]
    c_local = integrals.shape[3]
    nvirt = integrals.shape[4]
    rep_index = lax.axis_index("rep")
    col_index = lax.axis_index("col")
    occ_local = lax.dynamic_slice_in_dim(occ_irrep, rep_index * k_local, k_local)
    groups = jnp.arange(ngroup, dtype=jnp.int32)
    blocks = jnp.bitwise_xor(groups[:, None], occ_local[None, :])
    onehot = blocks[:, :, None] == groups[None, None, :]
    limit = jnp.sum(jnp.where(onehot, virt_count[None, None, :], 0), axis=2)
    c_global = col_index * c_local + jnp.arange(c_local, dtype=jnp.int32)
    c_live = c_global[None, None, :] < limit[:, :, None]
    places = jnp.arange(nvirt, dtype=jnp.int32)
    a_live = places[None, :] < virt_count[:, None]
    keep = c_live[:, None, :, :, None] & a_live[:, None, None, None, :]
    masked = jnp.where(keep, integrals, jnp.zeros_like(integrals))
    owned = ngroup // lax.axis_size("rep")
    partial_cycle = contract(masked, amplitudes)
    summed = lax.psum_scatter(partial_cycle, "rep", scatter_dimension=0, tiled=True)
    own_counts = lax.dynamic_slice_in_dim(virt_count, rep_index * owned, owned)
    b_live = places[None, :] < own_counts[:, None]
    result = jnp.where(b_live[:, None, None, None, :], summed, jnp.zeros_like(summed))
    return result.astype(jnp.bfloat16)


def solution(mesh):
    return jax.shard_map(
        body,
        mesh=mesh,
        in_specs=(P(None, "row", "rep", "col", None), P(None, "col", "rep", "row", None), P(), P()),
        out_specs=P("rep", "row", None, "col", None),
        check_vma=False,
    )
```

profile of v0, /device:TPU:1, one launch (start us, length us, event | category | flops | bytes accessed | tf_op | source)
XLA Modules:
  0.0 377.3 jit_solution(17503319874373990578)
XLA Ops:
  6.5 0.0 all-gather.3.cloned.1.call-start
  6.5 0.7 iota_compare_fusion.1
  7.3 0.7 dynamic_slice.7
  8.0 0.7 select_reduce_fusion
  8.7 0.1 broadcast_compare_fusion
  8.8 0.8 broadcast_and_fusion
  9.6 3.1 broadcast_select_fusion
  12.7 0.0 all-gather.3.cloned.1.call-update
  12.8 0.0 all-gather.5.cloned.1.call-start
  12.8 0.7 all-gather.5.cloned.1.call-update
  13.5 0.0 copy-start
  13.5 0.0 reduce-scatter.2.cloned.1.call-start
  13.6 84.3 %all-gather.3.cloned.1.call-done = bf16[8,2,15,128,128]{4,3,2,1,0:T(8,128)(2,1)} async-done(((bf16[8,2,15,32,128]{4,3,2,1,0:T(8,128)(2,1)}), bf16[8,2,15,128,128]{4,3,2,1,0:T(8,128)(2,1)}) %all-gather.3.cloned.1.call-update) | async-done | bytes 7864336 | tf_op jit(solution)/shard_map/all_gather | solution.py:8
  97.8 179.9 %all-gather.5.cloned.1.call-done = bf16[8,4,15,128,128]{4,3,2,1,0:T(8,128)(2,1)} async-done(((bf16[8,4,15,8,128]{4,3,2,1,0:T(8,128)(2,1)}), bf16[8,4,15,128,128]{4,3,2,1,0:T(8,128)(2,1)}) %all-gather.5.cloned.1.call-update) | async-done | bytes 15728656 | tf_op jit(solution)/shard_map/all_gather | solution.py:12
  277.7 14.3 %fusion.3 = f32[8,2,128,4,128]{4,2,3,1,0:T(8,128)} fusion(bf16[8,4,15,128,128]{4,3,2,1,0:T(8,128)(2,1)} %all-gather.5.cloned.1.call-done, bf16[8,2,15,128,128]{4,3,2,1,0:T(8,128)(2,1)} %all-gather.3.cloned.1.call-done), kind=kOutput, calls=%fused_computation.3 | convolution fusion | flops 4026531840 | bytes 27787264 | tf_op jit(solution)/shard_map/gikca,gjkcb->giajb/dot_general | solution.py:9
  292.0 0.0 reduce-scatter.2.cloned.1.call-update
  292.1 0.0 copy-done
  292.1 0.1 dynamic_slice.6
  292.2 0.1 iota_compare_fusion.2
  292.2 76.0 %reduce-scatter.2.cloned.1.call-done = f32[2,2,128,4,128]{4,2,3,1,0:T(8,128)} async-done(((f32[8,2,128,4,128]{4,2,3,1,0:T(8,128)}), f32[2,2,128,4,128]{4,2,3,1,0:T(8,128)}) %reduce-scatter.2.cloned.1.call-update) | async-done | bytes 1048592 | tf_op jit(solution)/shard_map/reduce_scatter | solution.py:37
  368.2 1.3 select_convert_fusion
  369.6 1.2 copy.6
  (2 shorter events, 0.0 us)
Async XLA Ops:
  6.5 91.3 %all-gather.3.cloned.1.call-start = ((), (), s32[]{:S(2)}) async-start(), calls=%async_computation.1 | async-start | bytes 9830400 | tf_op jit(solution)/shard_map/all_gather | solution.py:8
  12.8 265.0 %all-gather.5.cloned.1.call-start = ((), (), s32[]{:S(2)}) async-start(), calls=%async_computation.2 | async-start | bytes 16711680 | tf_op jit(solution)/shard_map/all_gather | solution.py:12
  13.5 278.6 %copy-start = (s32[8]{0:T(128)S(1)}, s32[8]{0:T(128)}, u32[]{:S(2)}) copy-start(s32[8]{0:T(128)} %param.6) | copy-start | bytes 100
  13.5 354.7 %reduce-scatter.2.cloned.1.call-start = ((), (), s32[]{:S(2)}) async-start(), calls=%async_computation.3 | async-start | bytes 5242880 | tf_op jit(solution)/shard_map/reduce_scatter | solution.py:37
Sparse Core Ops, SparseCore 0:
  12.9 84.8 all-gather.2
  100.4 177.3 all-gather.4
  292.2 75.9 reduce-scatter.1
where the time goes:
time: 377 us
  waiting for transfers between devices  341 us (90%)
  matrix products  14.3 us (4%)
  between operations  13.2 us (4%)
  other arithmetic  6.86 us (2%)
    all_gather x1, waiting for transfers between devices, contract(): lax.all_gather(t_part, 'row', axis=3, tiled=True)  180 us
    all_gather x1, waiting for transfers between devices, contract(): w_full = lax.all_gather(w_part, 'col', axis=3, tiled=True)  84.3 us
    reduce_scatter x1, waiting for transfers between devices, body(): lax.psum_scatter(partial_cycle, 'rep', scatter_dimension=0, tiled=True)  76 us
    dot_general x1, matrix products, contract(): jnp.einsum('gikca,gjkcb->giajb', w_full, lax.all_gather(t_part, 'row', ax...  14.3 us
  transfers between devices with their start and end apart: 3, of which 3 were waited for; matrix products, arithmetic and copies ran while one was open for 0% of the time, Pallas kernels for 0%

commit v1 on v0

--- a/solution.py
+++ b/solution.py
@@ -4,8 +4,29 @@
 from jax.sharding import PartitionSpec as P
 
 
+def gather_around(array, axis, dim):
+    size, position, rows = (lax.axis_size(axis), lax.axis_index(axis), array.shape[dim])
+    right = [(i, (i + 1) % size) for i in range(size)]
+    left = [(i, (i - 1) % size) for i in range(size)]
+    whole = jnp.zeros((*array.shape[:dim], size * rows, *array.shape[dim + 1 :]), array.dtype)
+    whole = lax.dynamic_update_slice_in_dim(whole, array, position * rows, axis=dim)
+    from_left = from_right = array
+    middle = size // 2
+    for turn in range(1, middle + 1):
+        from_left = lax.ppermute(from_left, axis, right)
+        whole = lax.dynamic_update_slice_in_dim(
+            whole, from_left, (position - turn) % size * rows, axis=dim
+        )
+        if turn < size - middle:
+            from_right = lax.ppermute(from_right, axis, left)
+            whole = lax.dynamic_update_slice_in_dim(
+                whole, from_right, (position + turn) % size * rows, axis=dim
+            )
+    return whole
+
+
 def contract(w_part, t_part):
-    w_full = lax.all_gather(w_part, "col", axis=3, tiled=True)
+    w_full = gather_around(w_part, "col", 3)
     return jnp.einsum(
         "gikca,gjkcb->giajb",
         w_full,

time: 377 us -> 583 us (1.55); the launches traced: 377 us -> 572 us
  local copies, waits for them, and re-layouts: 2.01 us -> 409 us
  waiting for transfers between devices: 341 us -> 128 us
    dynamic_update_slice x0 -> x4, local copies, waits for them, and re-layouts: none -> 372 us  [the longest x2 198 us: gather_around(): lax.dynamic_update_slice_in_dim(whole, from_left, (position - turn) % siz...]
    all_gather x1, waiting for transfers between devices: 180 us -> 0.01 us  [contract(): lax.all_gather(t_part, 'row', axis=3, tiled=True)]
    all_gather x1 -> x0, waiting for transfers between devices: 84.3 us -> none  [contract(): w_full = lax.all_gather(w_part, 'col', axis=3, tiled=True)]
    ppermute x0 -> x3, waiting for transfers between devices: none -> 40.6 us  [the longest x2 40.6 us: gather_around(): from_left = lax.ppermute(from_left, axis, right)]
    ppermute x0 -> x3, local copies, waits for them, and re-layouts: none -> 23.8 us  [the longest x2 15.8 us: gather_around(): from_left = lax.ppermute(from_left, axis, right)]
    reduce_scatter x1, waiting for transfers between devices: 76 us -> 86.4 us  [body(): lax.psum_scatter(partial_cycle, 'rep', scatter_dimension=0, tiled=True)]
  transfers between devices with their start and end apart: 3 -> 5, of which waited for: 3 -> 2; matrix products, arithmetic and copies ran while one was open for 0% -> 72% of each run, Pallas kernels for 0% -> 0%
where the time goes in v1:
time: 583 us; the launch traced here: 572 us
  local copies, waits for them, and re-layouts  409 us (70%)
  waiting for transfers between devices  128 us (22%)
  between operations  13.5 us (2%)
  matrix products  11.5 us (2%)
    dynamic_update_slice x2, local copies, waits for them, and re-layouts, gather_around(): lax.dynamic_update_slice_in_dim(whole, from_left, (position - turn) % siz...  198 us
    dynamic_update_slice x1, local copies, waits for them, and re-layouts, gather_around(): lax.dynamic_update_slice_in_dim(whole, from_right, (position + turn) % si...  98.7 us
    reduce_scatter x1, waiting for transfers between devices, body(): lax.psum_scatter(partial_cycle, 'rep', scatter_dimension=0, tiled=True)  86.4 us
    dynamic_update_slice x1, local copies, waits for them, and re-layouts, gather_around(): lax.dynamic_update_slice_in_dim(whole, array, position * rows, axis=dim)  75.9 us
    ppermute x2, waiting for transfers between devices, gather_around(): from_left = lax.ppermute(from_left, axis, right)  40.6 us
    ppermute x2, local copies, waits for them, and re-layouts, gather_around(): from_left = lax.ppermute(from_left, axis, right)  15.8 us
  transfers between devices with their start and end apart: 5, of which 2 were waited for; matrix products, arithmetic and copies ran while one was open for 72% of the time, Pallas kernels for 0%

profile of v1, /device:TPU:1, one launch (start us, length us, event | category | flops | bytes accessed | tf_op | source)
XLA Modules:
  0.0 572.4 jit_solution(15484800934928311996)
XLA Ops:
  6.5 0.7 all-gather.2.cloned.1.call-update
  7.3 0.7 dynamic_slice.7
  8.0 0.7 select_reduce_fusion
  8.8 0.7 iota_compare_fusion.1
  9.5 0.1 broadcast_compare_fusion
  9.6 0.8 broadcast_and_fusion
  10.4 1.7 broadcast_select_fusion
  12.1 2.2 collective-permute-start
  14.3 1.5 collective-permute-start.1
  15.9 40.6 %collective-permute-done = bf16[8,2,15,32,128]{4,3,2,1,0:T(8,128)(2,1)} collective-permute-done((bf16[8,2,15,32,128]{4,3,2,1,0:T(8,128)(2,1)S(1)}, bf16[8,2,15,32,128]{4,3,2,1,0:T(8,128)(2,1)}, u32[]{:S(2)}, u32[]{:S(2)}) %collective-permute-start) | collective-permute-done | bytes 1966112 | tf_op jit(solution)/shard_map/ppermute | solution.py:16
  56.5 1.5 collective-permute-start.2
  58.0 5.7 copy.10
  63.7 5.2 broadcast_in_dim.32
  68.9 75.9 %dynamic_update_slice.12 = bf16[8,2,15,128,128]{3,4,2,1,0:T(8,128)(2,1)} dynamic-update-slice(bf16[8,2,15,128,128]{3,4,2,1,0:T(8,128)(2,1)} %broadcast_in_dim.32, bf16[8,2,15,32,128]{3,4,2,1,0:T(8,128)(2,1)} %copy.10, s32[]{:T(128)} %constant.38.clone.1, s32[]{:T(128)} %constant.38.clone.1, s32[]{:T(128)} %constant.38.clone.1, s32[]{:T(128)S(6)} %select_n.49, s32[]{:T(128)} %constant.38.clone.1) | dynamic-update-slice | bytes 3932164 | tf_op jit(solution)/shard_map/dynamic_update_slice | solution.py:12
  144.8 7.9 %copy.11 = bf16[8,2,15,32,128]{3,4,2,1,0:T(8,128)(2,1)} copy(bf16[8,2,15,32,128]{4,3,2,1,0:T(8,128)(2,1)} %collective-permute-done) | data formatting | bytes 3932160 | tf_op jit(solution)/shard_map/ppermute | solution.py:16
  152.7 98.8 %dynamic_update_slice.13 = bf16[8,2,15,128,128]{3,4,2,1,0:T(8,128)(2,1)} dynamic-update-slice(bf16[8,2,15,128,128]{3,4,2,1,0:T(8,128)(2,1)} %dynamic_update_slice.12, bf16[8,2,15,32,128]{3,4,2,1,0:T(8,128)(2,1)} %copy.11, s32[]{:T(128)} %constant.38.clone.1, s32[]{:T(128)} %constant.38.clone.1, s32[]{:T(128)} %constant.38.clone.1, s32[]{:T(128)S(6)} %select_n.51, s32[]{:T(128)} %constant.38.clone.1) | dynamic-update-slice | bytes 3932164 | tf_op jit(solution)/shard_map/dynamic_update_slice | solution.py:17
  251.6 7.9 %copy.12 = bf16[8,2,15,32,128]{3,4,2,1,0:T(8,128)(2,1)} copy(bf16[8,2,15,32,128]{4,3,2,1,0:T(8,128)(2,1)} %collective-permute-done.1) | data formatting | bytes 3932160 | tf_op jit(solution)/shard_map/ppermute | solution.py:21
  259.5 98.7 %dynamic_update_slice.14 = bf16[8,2,15,128,128]{3,4,2,1,0:T(8,128)(2,1)} dynamic-update-slice(bf16[8,2,15,128,128]{3,4,2,1,0:T(8,128)(2,1)} %dynamic_update_slice.13, bf16[8,2,15,32,128]{3,4,2,1,0:T(8,128)(2,1)} %copy.12, s32[]{:T(128)} %constant.38.clone.1, s32[]{:T(128)} %constant.38.clone.1, s32[]{:T(128)} %constant.38.clone.1, s32[]{:T(128)S(6)} %select_n.53, s32[]{:T(128)} %constant.38.clone.1) | dynamic-update-slice | bytes 3932164 | tf_op jit(solution)/shard_map/dynamic_update_slice | solution.py:22
  358.2 7.9 %copy.13 = bf16[8,2,15,32,128]{3,4,2,1,0:T(8,128)(2,1)} copy(bf16[8,2,15,32,128]{4,3,2,1,0:T(8,128)(2,1)} %collective-permute-done.2) | data formatting | bytes 3932160 | tf_op jit(solution)/shard_map/ppermute | solution.py:16
  366.1 98.7 %dynamic_update_slice.15 = bf16[8,2,15,128,128]{3,4,2,1,0:T(8,128)(2,1)} dynamic-update-slice(bf16[8,2,15,128,128]{3,4,2,1,0:T(8,128)(2,1)} %dynamic_update_slice.14, bf16[8,2,15,32,128]{3,4,2,1,0:T(8,128)(2,1)} %copy.13, s32[]{:T(128)} %constant.38.clone.1, s32[]{:T(128)} %constant.38.clone.1, s32[]{:T(128)} %constant.38.clone.1, s32[]{:T(128)S(6)} %select_n.55, s32[]{:T(128)} %constant.38.clone.1) | dynamic-update-slice | bytes 3932164 | tf_op jit(solution)/shard_map/dynamic_update_slice | solution.py:17
  464.9 11.5 %fusion.3 = f32[8,2,128,4,128]{4,2,3,1,0:T(8,128)} fusion(bf16[8,4,15,128,128]{4,3,2,1,0:T(8,128)(2,1)} %all-gather.2.cloned.1.call-done, bf16[8,2,15,128,128]{3,4,2,1,0:T(8,128)(2,1)} %dynamic_update_slice.15), kind=kOutput, calls=%fused_computation.3 | convolution fusion | flops 4026531840 | bytes 27787264 | tf_op jit(solution)/shard_map/gikca,gjkcb->giajb/dot_general | solution.py:30
  476.5 86.4 %reduce-scatter.2.cloned.1.call-done = f32[2,2,128,4,128]{4,2,3,1,0:T(8,128)} async-done(((f32[8,2,128,4,128]{4,2,3,1,0:T(8,128)}), f32[2,2,128,4,128]{4,2,3,1,0:T(8,128)}) %reduce-scatter.2.cloned.1.call-update) | async-done | bytes 1048592 | tf_op jit(solution)/shard_map/reduce_scatter | solution.py:58
  563.0 1.3 select_convert_fusion
  564.3 1.2 copy.14
  (12 shorter events, 0.2 us)
Async XLA Ops:
  6.5 458.3 %all-gather.2.cloned.1.call-start = ((), (), s32[]{:S(2)}) async-start(), calls=%async_computation.1 | async-start | bytes 16711680 | tf_op jit(solution)/shard_map/all_gather | solution.py:33
  7.3 555.7 %reduce-scatter.2.cloned.1.call-start = ((), (), s32[]{:S(2)}) async-start(), calls=%async_computation.2 | async-start | bytes 5242880 | tf_op jit(solution)/shard_map/reduce_scatter | solution.py:58
  12.1 44.3 %collective-permute-start = (bf16[8,2,15,32,128]{4,3,2,1,0:T(8,128)(2,1)S(1)}, bf16[8,2,15,32,128]{4,3,2,1,0:T(8,128)(2,1)}, u32[]{:S(2)}, u32[]{:S(2)}) collective-permute-start(bf16[8,2,15,32,128]{4,3,2,1,0:T(8,128)(2,1)S(1)} %broadcast_select_fusion), channel_id=1, source_target_pairs={{0,4},{4,8},{8,12},{12,0},{1,5},{5,9},{9,13},{13,1},{2,6},{6,10},{... | collective-permute-start | bytes 5898248 | tf_op jit(solution)/shard_map/ppermute | solution.py:16
  14.3 237.3 %collective-permute-start.1 = (bf16[8,2,15,32,128]{4,3,2,1,0:T(8,128)(2,1)S(1)}, bf16[8,2,15,32,128]{4,3,2,1,0:T(8,128)(2,1)}, u32[]{:S(2)}, u32[]{:S(2)}) collective-permute-start(bf16[8,2,15,32,128]{4,3,2,1,0:T(8,128)(2,1)S(1)} %broadcast_select_fusion), channel_id=1, source_target_pairs={{0,12},{4,0},{8,4},{12,8},{1,13},{5,1},{9,5},{13,9},{2,14},{6,2},{... | collective-permute-start | bytes 5898248 | tf_op jit(solution)/shard_map/ppermute | solution.py:21
  56.5 301.7 %collective-permute-start.2 = (bf16[8,2,15,32,128]{4,3,2,1,0:T(8,128)(2,1)}, bf16[8,2,15,32,128]{4,3,2,1,0:T(8,128)(2,1)}, u32[]{:S(2)}, u32[]{:S(2)}) collective-permute-start(bf16[8,2,15,32,128]{4,3,2,1,0:T(8,128)(2,1)} %collective-permute-done), channel_id=1, source_target_pairs={{0,4},{4,8},{8,12},{12,0},{1,5},{5,9},{9,13},{13,1},{2,6},{6,10},{... | collective-permute-start | bytes 5898248 | tf_op jit(solution)/shard_map/ppermute | solution.py:16
  464.9 11.5 %copy-start = (s32[8]{0:T(128)S(1)}, s32[8]{0:T(128)}, u32[]{:S(2)}) copy-start(s32[8]{0:T(128)} %param.6) | copy-start | bytes 100
Sparse Core Ops, SparseCore 0:
  9.9 180.1 all-gather.1
  476.5 86.4 reduce-scatter.1
